TPU v7x, 512 devices: a whole 4x4x16 slice. The times are simulated.
512 devices in a mesh: inst: 16 (over y_lo, x, core), blk: 32 (over z, y_hi).
Axes of the slice: x: 4, y: 4 (y_hi: 2, y_lo: 2; y = y_hi * 2 + y_lo), z: 16, core: 2. Of those that a mesh axis runs over, the one named last changes fastest.
Arguments:
- state: float32 [16, 2, 6, 8, 8, 4096], P('inst', None, None, None, None, 'blk'), may hold values from -0.5 to 3, as said below
- donor_block: int32 [16, 2, 32], P('inst', None, 'blk'), may hold values from 0 to 31, as said below
- donor_offset: int32 [16, 2, 32], P('inst', None, 'blk'), may hold values from 0 to 127, as said below
Outputs:
- hb_residual: float32 [16, 2, 6, 8, 8, 4096], P('inst', None, None, None, None, 'blk')
- new_state: float32 [16, 2, 6, 8, 8, 4096], P('inst', None, None, None, None, 'blk')
Inputs may be any that keep to these rules, and one draw needn't show every extreme that they name: For each instance n and row r there is one rotation R with donor_block[n, r, b] = (b + R) mod 32 for every block b. `donor_offset`: for each instance and row the offset is the same for all blocks. `state`: density lies in [0.8, 1.25], momenta in [-0.5, 0.5], total energy in [2, 3], turbulence variable in [0.05, 0.5].
All inputs are finite; a program needn't handle non-finite values.
Results may differ from a plain program's by a relative error of at most 0.0003.
Values sent between devices are 32-bit elements; how exact they have to be, the bound alone decides.
No kernel may reach another device: no remote copies, remote signals or barrier semaphores. Data moves between devices by JAX's collectives and lax.ppermute only.
A program may use at most 64 MiB of HBM per device.

v0:
```python
import jax
import jax.numpy as jnp
from jax import lax
from jax.sharding import PartitionSpec as P

gamma_ratio = 1.4
second_coef = 0.5
fourth_coef = 1.0 / 32.0
courant = 0.8
frequency = 0.5
highest = lax.Precision.HIGHEST


def padded_2(block, sides, width):
    for axis, dim in sides:
        count = lax.axis_size(axis)
        forward = [(i, i + 1) for i in range(count - 1)]
        forward.append((count - 1, 0))
        backward = [(target, source) for source, target in forward]
        low = lax.ppermute(
            lax.slice_in_dim(block, block.shape[dim] - width, None, axis=dim), axis, forward
        )
        high = lax.ppermute(lax.slice_in_dim(block, 0, width, axis=dim), axis, backward)
        block = jnp.concatenate([low, block, high], axis=dim)
    return block


def spectral_weights(target, source, number):
    distance = jnp.mod(target - source, number)
    angle = jnp.pi / number * distance.astype(jnp.float32)
    parity = 1.0 - 2.0 * jnp.mod(distance, 2).astype(jnp.float32)
    nonzero = distance != 0
    sine_safe = jnp.where(nonzero, jnp.sin(angle), 1.0)
    cotangent = jnp.where(nonzero, jnp.cos(angle) / sine_safe, 0.0)
    return parity * (0.25 * frequency + 0.5 * frequency * cotangent)


def take_range(array, begin, length, along):
    return lax.slice_in_dim(array, begin, begin + length, axis=along)


def flux_divergence(extended, along):
    length = extended.shape[along] - 4
    cell_axis = along - 1
    density = extended[0]
    inverse = 1.0 / density
    normal_vel = extended[along] * inverse
    kinetic = 0.5 * (extended[1] ** 2 + extended[2] ** 2 + extended[3] ** 2) * inverse
    pressure = (gamma_ratio - 1.0) * (extended[4] - kinetic)
    sound = jnp.sqrt(gamma_ratio * pressure * inverse)
    momentum_flux = []
    for component in (1, 2, 3):
        if component == along:
            momentum_flux.append(extended[component] * normal_vel + pressure)
        else:
            momentum_flux.append(extended[component] * normal_vel)
    fluxes = jnp.stack(
        [extended[along]]
        + momentum_flux
        + [(extended[4] + pressure) * normal_vel, extended[5] * normal_vel]
    )
    radius = jnp.abs(normal_vel) + sound
    p_plus = take_range(pressure, 2, length + 2, cell_axis)
    p_here = take_range(pressure, 1, length + 2, cell_axis)
    p_minus = take_range(pressure, 0, length + 2, cell_axis)
    sensor = jnp.abs(p_plus - 2.0 * p_here + p_minus) / (p_plus + 2.0 * p_here + p_minus)
    spread = 0.5 * (
        take_range(radius, 1, length + 1, cell_axis) + take_range(radius, 2, length + 1, cell_axis)
    )
    eps_two = second_coef * jnp.maximum(
        take_range(sensor, 0, length + 1, cell_axis), take_range(sensor, 1, length + 1, cell_axis)
    )
    eps_four = jnp.maximum(0.0, fourth_coef - eps_two)
    first_diff = take_range(extended, 2, length + 1, along) - take_range(
        extended, 1, length + 1, along
    )
    third_diff = (
        take_range(extended, 3, length + 1, along)
        - 3.0 * take_range(extended, 2, length + 1, along)
        + 3.0 * take_range(extended, 1, length + 1, along)
        - take_range(extended, 0, length + 1, along)
    )
    interface = 0.5 * (
        take_range(fluxes, 1, length + 1, along) + take_range(fluxes, 2, length + 1, along)
    ) - spread * (eps_two * first_diff - eps_four * third_diff)
    return take_range(interface, 1, length, along) - take_range(interface, 0, length, along)


def wall_extend(block):
    mirror_sign = jnp.array([1.0, 1.0, -1.0, 1.0, 1.0, 1.0], jnp.float32).reshape(6, 1, 1, 1)
    lower_ghost = block[:, :, 0:2][:, :, ::-1] * mirror_sign
    upper_ghost = block[:, :, -2:][:, :, ::-1] * mirror_sign
    return jnp.concatenate([lower_ghost, block, upper_ghost], axis=2)


def row_residual(block, low_ghost, high_ghost, circum_ext):
    axial_ext = jnp.concatenate([low_ghost, block, high_ghost], axis=1)
    return (
        flux_divergence(axial_ext, 1)
        + flux_divergence(wall_extend(block), 2)
        + flux_divergence(circum_ext, 3)
    )


def local_step(fields, number):
    inverse = 1.0 / fields[:, 0]
    kinetic = 0.5 * (fields[:, 1] ** 2 + fields[:, 2] ** 2 + fields[:, 3] ** 2) * inverse
    pressure = (gamma_ratio - 1.0) * (fields[:, 4] - kinetic)
    sound = jnp.sqrt(gamma_ratio * pressure * inverse)
    speeds = (jnp.abs(fields[:, 1]) + jnp.abs(fields[:, 2]) + jnp.abs(fields[:, 3])) * inverse
    return courant / (speeds + 3.0 * sound + frequency * number / 2.0)


def donor_faces(all_faces, donor, shift_cells, total_blocks, width):
    first_face = lax.dynamic_index_in_dim(all_faces, donor, 0, keepdims=False)
    second_face = lax.dynamic_index_in_dim(
        all_faces, jnp.mod(donor + 1, total_blocks), 0, keepdims=False
    )
    joined = jnp.concatenate([first_face, second_face], axis=3)
    return lax.dynamic_slice_in_dim(joined, shift_cells, width, axis=3)


def per_device(state, donor_block, donor_offset):
    number = lax.axis_size("inst")
    total_blocks = lax.axis_size("blk")
    own_instance = lax.axis_index("inst")
    fields = state[0]
    width = fields.shape[-1]
    padded = padded_2(state, (("blk", 5),), 2)[0]
    outlet = state[:, 0, :, -2:]
    inlet = state[:, 1, :, 0:2]
    outlet_all, inlet_all = (
        lax.all_gather(outlet, "blk", axis=0, tiled=True),
        lax.all_gather(inlet, "blk", axis=0, tiled=True),
    )
    rotor_high = donor_faces(
        inlet_all, donor_block[0, 0, 0], donor_offset[0, 0, 0], total_blocks, width
    )
    stator_low = donor_faces(
        outlet_all, donor_block[0, 1, 0], donor_offset[0, 1, 0], total_blocks, width
    )
    piece = lax.all_gather(state, "inst", axis=0, tiled=True)
    sources = jnp.arange(piece.shape[0], dtype=jnp.int32)
    weights = spectral_weights(own_instance, sources, number)
    spectral = jnp.tensordot(weights, piece, axes=(0, 0), precision=highest)
    rotor = fields[0]
    stator = fields[1]
    rotor_low = jnp.concatenate([rotor[:, 0:1], rotor[:, 0:1]], axis=1)
    stator_high = jnp.concatenate([stator[:, -1:], stator[:, -1:]], axis=1)
    rotor_res = row_residual(rotor, rotor_low, rotor_high, padded[0])
    stator_res = row_residual(stator, stator_low, stator_high, padded[1])
    residual = jnp.stack([rotor_res, stator_res]) + spectral
    step = local_step(fields, number)
    updated = fields - step[:, None] * residual
    return (residual[None], updated[None])


def solution(mesh):
    return jax.shard_map(
        per_device,
        mesh=mesh,
        in_specs=(
            P("inst", None, None, None, None, "blk"),
            P("inst", None, "blk"),
            P("inst", None, "blk"),
        ),
        out_specs=(
            P("inst", None, None, None, None, "blk"),
            P("inst", None, None, None, None, "blk"),
        ),
        check_vma=False,
    )
```

profile of v0, /device:TPU:1, one launch (start us, length us, event | category | flops | bytes accessed | tf_op | source)
XLA Modules:
  0.0 371.4 jit_solution(17688199115417346570)
XLA Ops:
  7.2 1.5 fusion.181
  8.8 0.7 all-gather.10.cloned.1.call-update
  9.6 0.7 all-gather.6.cloned.1.call-update
  10.3 1.3 fusion.182
  11.5 5.6 %collective-permute-start = (f32[1,2,6,8,8,2]{5,4,3,2,1,0:T(8,128)S(1)}, f32[1,2,6,8,8,2]{5,4,3,2,1,0:T(8,128)S(1)}, u32[]{:S(2)}, u32[]{:S(2)}) collective-permute-start(f32[1,2,6,8,8,2]{5,4,3,2,1,0:T(8,128)S(1)} %get-tuple-element.69), channel_id=1, source_target_pairs={{0,1},{1,2},{2,3},{3,4},{4,5},{5,6},{6,7},{7,8},{8,9},{9,10},{10,1... | collective-permute-start | bytes 18440 | tf_op jit(solution)/shard_map/ppermute | solution.py:20
  17.2 10.9 %collective-permute-start.1 = (f32[1,2,6,8,8,2]{5,4,3,2,1,0:T(8,128)S(1)}, f32[1,2,6,8,8,2]{5,4,3,2,1,0:T(8,128)S(1)}, u32[]{:S(2)}, u32[]{:S(2)}) collective-permute-start(f32[1,2,6,8,8,2]{5,4,3,2,1,0:T(8,128)S(1)} %get-tuple-element.70), channel_id=1, source_target_pairs={{1,0},{2,1},{3,2},{4,3},{5,4},{6,5},{7,6},{8,7},{9,8},{10,9},{11,1... | collective-permute-start | bytes 18440 | tf_op jit(solution)/shard_map/ppermute | solution.py:23
  28.0 1.1 slice_bitcast_fusion.3
  29.2 0.1 rev.13
  29.3 0.1 rev.12
  29.4 0.1 rev.15
  29.5 0.1 rev.14
  29.7 0.8 broadcast_multiply_fusion.6
  30.5 0.1 pad_maximum_fusion.5
  30.8 0.7 fusion.111
  32.0 0.6 fusion.185
  32.6 0.4 fusion.26
  33.0 0.4 fusion.12
  33.4 0.6 fusion.186
  40.6 0.6 slice.693
  41.2 0.6 slice.758
  44.4 0.4 pad_maximum_fusion
  45.3 0.1 add_divide_fusion
  45.9 1.1 fusion.5
  47.0 107.0 %all-gather.8.cloned.1.call-done = f32[32,1,6,2,8,128]{5,4,3,2,1,0:T(8,128)} async-done(((f32[1,1,6,2,8,128]{5,4,3,2,1,0:T(8,128)}), f32[32,1,6,2,8,128]{5,4,3,2,1,0:T(8,128)}) %all-gather.8.cloned.1.call-update) | async-done | bytes 1572880 | tf_op jit(solution)/shard_map/all_gather | solution.py:134
  153.9 0.8 dynamic-slice_bitcast_fusion.2
  154.9 143.0 %all-gather.10.cloned.1.call-done = f32[32,1,6,2,8,128]{5,4,3,2,1,0:T(8,128)} async-done(((f32[1,1,6,2,8,128]{5,4,3,2,1,0:T(8,128)}), f32[32,1,6,2,8,128]{5,4,3,2,1,0:T(8,128)}) %all-gather.10.cloned.1.call-update) | async-done | bytes 1572880 | tf_op jit(solution)/shard_map/all_gather | solution.py:133
  297.8 0.8 dynamic-slice_bitcast_fusion
  299.6 0.1 fusion.53
  299.7 0.1 fusion.50
  299.8 54.4 %all-gather.6.cloned.1.call-done = f32[16,2,6,8,8,128]{5,4,3,2,1,0:T(8,128)} async-done(((f32[1,2,6,8,8,128]{5,4,3,2,1,0:T(8,128)}), f32[16,2,6,8,8,128]{5,4,3,2,1,0:T(8,128)}) %all-gather.6.cloned.1.call-update) | async-done | bytes 6291472 | tf_op jit(solution)/shard_map/all_gather | solution.py:142
  354.2 9.6 %fusion = f32[1,2,6,8,8,128]{5,0,4,3,2,1:T(1,128)S(1)} fusion(f32[16,2,6,8,8,128]{5,4,3,2,1,0:T(8,128)} %all-gather.6.cloned.1.call-done, s32[]{:T(128)S(6)} %axis_index.15), kind=kOutput, calls=%fused_computation | convolution fusion | flops 18874928 | bytes 6684676 | tf_op jit(solution)/shard_map/dot_general | solution.py:145
  363.9 1.0 subtract_bitcast_fusion
  (86 shorter events, 2.3 us)
Async XLA Ops:
  7.2 23.6 %copy-start = (f32[1,2,6,8,8,128]{5,4,3,2,1,0:T(8,128)S(1)}, f32[1,2,6,8,8,128]{5,4,3,2,1,0:T(8,128)}, u32[]{:S(2)}) copy-start(f32[1,2,6,8,8,128]{5,4,3,2,1,0:T(8,128)} %param.5) | copy-start | bytes 1179652
  7.2 24.8 %copy-start.4 = (s32[1,2,1]{1,2,0:T(1,128)S(1)}, s32[1,2,1]{1,2,0:T(1,128)}, u32[]{:S(2)}) copy-start(s32[1,2,1]{1,2,0:T(1,128)} %param.6) | copy-start | bytes 28
  7.2 146.7 %all-gather.8.cloned.1.call-start = ((), (), s32[]{:S(2)}) async-start(), calls=%async_computation.1 | async-start | bytes 1622016 | tf_op jit(solution)/shard_map/all_gather | solution.py:134
  8.8 289.1 %all-gather.10.cloned.1.call-start = ((), (), s32[]{:S(2)}) async-start(), calls=%async_computation.2 | async-start | bytes 1622016 | tf_op jit(solution)/shard_map/all_gather | solution.py:133
  9.5 344.7 %all-gather.6.cloned.1.call-start = ((), (), s32[]{:S(2)}) async-start(), calls=%async_computation | async-start | bytes 6684672 | tf_op jit(solution)/shard_map/all_gather | solution.py:142
  11.5 32.8 %collective-permute-start = (f32[1,2,6,8,8,2]{5,4,3,2,1,0:T(8,128)S(1)}, f32[1,2,6,8,8,2]{5,4,3,2,1,0:T(8,128)S(1)}, u32[]{:S(2)}, u32[]{:S(2)}) collective-permute-start(f32[1,2,6,8,8,2]{5,4,3,2,1,0:T(8,128)S(1)} %get-tuple-element.69), channel_id=1, source_target_pairs={{0,1},{1,2},{2,3},{3,4},{4,5},{5,6},{6,7},{7,8},{8,9},{9,10},{10,1... | collective-permute-start | bytes 18440 | tf_op jit(solution)/shard_map/ppermute | solution.py:20
  17.2 27.2 %collective-permute-start.1 = (f32[1,2,6,8,8,2]{5,4,3,2,1,0:T(8,128)S(1)}, f32[1,2,6,8,8,2]{5,4,3,2,1,0:T(8,128)S(1)}, u32[]{:S(2)}, u32[]{:S(2)}) collective-permute-start(f32[1,2,6,8,8,2]{5,4,3,2,1,0:T(8,128)S(1)} %get-tuple-element.70), channel_id=1, source_target_pairs={{1,0},{2,1},{3,2},{4,3},{5,4},{6,5},{7,6},{8,7},{9,8},{10,9},{11,1... | collective-permute-start | bytes 18440 | tf_op jit(solution)/shard_map/ppermute | solution.py:23
  29.1 4.2 %copy-start.5 = (s32[1,2,1]{1,2,0:T(1,128)S(1)}, s32[1,2,1]{1,2,0:T(1,128)}, u32[]{:S(2)}) copy-start(s32[1,2,1]{1,2,0:T(1,128)} %param.7) | copy-start | bytes 28
  45.1 253.6 %copy-start.2 = (f32[6,1,8,128]{3,2,1,0:T(8,128)S(1)}, f32[6,1,8,128]{3,2,1,0:T(8,128)}, u32[]{:S(2)}) copy-start(f32[6,1,8,128]{3,2,1,0:T(8,128)} %slice.758) | copy-start | bytes 73732
  45.1 253.6 %copy-start.3 = (f32[6,1,8,128]{3,2,1,0:T(8,128)S(1)}, f32[6,1,8,128]{3,2,1,0:T(8,128)}, u32[]{:S(2)}) copy-start(f32[6,1,8,128]{3,2,1,0:T(8,128)} %slice.693) | copy-start | bytes 73732
  299.2 64.7 %copy-start.1 = (f32[2,8,8,128]{3,2,1,0:T(8,128)S(1)}, f32[2,8,8,128]{3,2,1,0:T(8,128)}, u32[]{:S(2)}) copy-start(f32[2,8,8,128]{3,2,1,0:T(8,128)} %fusion.111) | copy-start | bytes 196612
Sparse Core Ops, SparseCore 0:
  11.7 142.2 all-gather.7
  157.0 140.7 all-gather.9
  300.0 54.2 all-gather.5
where the time goes:
time: 372 us; the launch traced here: 371 us
  waiting for transfers between devices  306 us (82%)
  between operations  23.6 us (6%)
  starting transfers between devices  16.6 us (4%)
  matrix products  9.63 us (3%)
  local copies, waits for them, and re-layouts  8.67 us (2%)
  other arithmetic  7.18 us (2%)
    all_gather x1, waiting for transfers between devices, per_device(): lax.all_gather(outlet, 'blk', axis=0, tiled=True)  143 us
    all_gather x1, waiting for transfers between devices, per_device(): lax.all_gather(inlet, 'blk', axis=0, tiled=True)  107 us
    all_gather x1, waiting for transfers between devices, per_device(): piece = lax.all_gather(state, 'inst', axis=0, tiled=True)  54.4 us
    ppermute x1, starting transfers between devices, padded_2(): lax.ppermute(lax.slice_in_dim(block, 0, width, axis=dim), axis, backward)  10.9 us
    dot_general x1, matrix products, per_device(): spectral = jnp.tensordot(weights, piece, axes=(0, 0), precision=highest)  9.63 us
  transfers between devices with their start and end apart: 5, of which 3 were waited for; matrix products, arithmetic and copies ran while one was open for 4% of the time, Pallas kernels for 0%

commit v1 on v0

--- a/solution.py
+++ b/solution.py
@@ -129,8 +129,17 @@
     padded = padded_2(state, (("blk", 5),), 2)[0]
     outlet = state[:, 0, :, -2:]
     inlet = state[:, 1, :, 0:2]
+    define_the_routes_all = lambda point, chip_axis: jnp.concatenate(
+        jax.lax.all_to_all(
+            jnp.stack(jax.lax.axis_size(chip_axis) * [point], axis=0),
+            axis_name=chip_axis,
+            split_axis=0,
+            concat_axis=0,
+        ),
+        0,
+    )
     outlet_all, inlet_all = (
-        lax.all_gather(outlet, "blk", axis=0, tiled=True),
+        define_the_routes_all(outlet, "blk"),
         lax.all_gather(inlet, "blk", axis=0, tiled=True),
     )
     rotor_high = donor_faces(

time: 372 us -> 241 us (0.65)
  waiting for transfers between devices: 306 us -> 163 us
  starting transfers between devices: 16.6 us -> 25.6 us
    all_gather x1 -> x0, waiting for transfers between devices: 143 us -> none  [per_device(): lax.all_gather(outlet, 'blk', axis=0, tiled=True)]
    all_to_all x0 -> x1, starting transfers between devices: none -> 9.08 us  [per_device(): jax.lax.all_to_all(jnp.stack(jax.lax.axis_size(chip_axis) * [point], axis...]
  transfers between devices with their start and end apart: 5 -> 5, of which waited for: 3 -> 2; matrix products, arithmetic and copies ran while one was open for 4% -> 7% of each run, Pallas kernels for 0% -> 0%
where the time goes in v1:
time: 241 us
  waiting for transfers between devices  163 us (68%)
  starting transfers between devices  25.6 us (11%)
  between operations  23.6 us (10%)
  other arithmetic  10.7 us (4%)
  matrix products  9.63 us (4%)
  local copies, waits for them, and re-layouts  8.15 us (3%)
    all_gather x1, waiting for transfers between devices, per_device(): lax.all_gather(inlet, 'blk', axis=0, tiled=True)  110 us
    all_gather x1, waiting for transfers between devices, per_device(): piece = lax.all_gather(state, 'inst', axis=0, tiled=True)  52 us
    ppermute x1, starting transfers between devices, padded_2(): lax.ppermute(lax.slice_in_dim(block, 0, width, axis=dim), axis, backward)  10.9 us
    dot_general x1, matrix products, per_device(): spectral = jnp.tensordot(weights, piece, axes=(0, 0), precision=highest)  9.63 us
    all_to_all x1, starting transfers between devices, per_device(): jax.lax.all_to_all(jnp.stack(jax.lax.axis_size(chip_axis) * [point], axis...  9.08 us
    ppermute x1, starting transfers between devices, padded_2(): lax.ppermute(lax.slice_in_dim(block, block.shape[dim] - width, None, axis...  5.64 us
  transfers between devices with their start and end apart: 5, of which 2 were waited for; matrix products, arithmetic and copies ran while one was open for 7% of the time, Pallas kernels for 0%

profile of v1, /device:TPU:1, one launch (start us, length us, event | category | flops | bytes accessed | tf_op | source)
XLA Modules:
  0.0 240.7 jit_solution(2549283254433945969)
XLA Ops:
  7.2 1.5 fusion.181
  8.8 0.7 all-gather.4.cloned.1.call-update
  9.5 1.3 fusion.182
  10.8 5.6 %collective-permute-start = (f32[1,2,6,8,8,2]{5,4,3,2,1,0:T(8,128)S(1)}, f32[1,2,6,8,8,2]{5,4,3,2,1,0:T(8,128)}, u32[]{:S(2)}, u32[]{:S(2)}) collective-permute-start(f32[1,2,6,8,8,2]{5,4,3,2,1,0:T(8,128)S(1)} %get-tuple-element.69), channel_id=1, source_target_pairs={{0,1},{1,2},{2,3},{3,4},{4,5},{5,6},{6,7},{7,8},{8,9},{9,10},{10,1... | collective-permute-start | bytes 18440 | tf_op jit(solution)/shard_map/ppermute | solution.py:20
  16.4 10.9 %collective-permute-start.1 = (f32[1,2,6,8,8,2]{5,4,3,2,1,0:T(8,128)S(1)}, f32[1,2,6,8,8,2]{5,4,3,2,1,0:T(8,128)}, u32[]{:S(2)}, u32[]{:S(2)}) collective-permute-start(f32[1,2,6,8,8,2]{5,4,3,2,1,0:T(8,128)S(1)} %get-tuple-element.70), channel_id=1, source_target_pairs={{1,0},{2,1},{3,2},{4,3},{5,4},{6,5},{7,6},{8,7},{9,8},{10,9},{11,1... | collective-permute-start | bytes 18440 | tf_op jit(solution)/shard_map/ppermute | solution.py:23
  27.3 1.4 stack.24
  28.7 9.1 %all-to-all-start = ((f32[32,1,6,2,8,128]{5,4,3,2,1,0:T(8,128)}), f32[32,1,6,2,8,128]{5,4,3,2,1,0:T(8,128)S(1)}, u32[]{:S(2)}, u32[]{:S(2)}) async-start(f32[32,1,6,2,8,128]{5,4,3,2,1,0:T(8,128)} %stack.24), calls=%async_computation | async-start | bytes 3145728 | tf_op jit(solution)/shard_map/all_to_all | solution.py:133
  37.9 0.1 rev.13
  38.0 0.1 rev.12
  38.2 0.1 rev.15
  38.3 0.1 rev.14
  38.4 0.1 broadcast_multiply_fusion.6
  38.5 0.1 pad_maximum_fusion.5
  38.9 0.7 fusion.111
  40.0 0.6 fusion.185
  40.7 0.4 fusion.26
  41.0 1.1 fusion.12
  42.1 0.6 fusion.186
  49.1 0.6 slice.696
  49.7 0.6 slice.761
  52.9 1.5 pad_maximum_fusion
  55.5 1.1 fusion.5
  56.5 110.4 %all-gather.6.cloned.1.call-done = f32[32,1,6,2,8,128]{5,4,3,2,1,0:T(8,128)} async-done(((f32[1,1,6,2,8,128]{5,4,3,2,1,0:T(8,128)}), f32[32,1,6,2,8,128]{5,4,3,2,1,0:T(8,128)}) %all-gather.6.cloned.1.call-update) | async-done | bytes 1572880 | tf_op jit(solution)/shard_map/all_gather | solution.py:143
  166.9 0.8 dynamic-slice_bitcast_fusion
  167.7 0.7 fusion.113
  168.6 0.9 pad_maximum_fusion.11
  170.0 1.0 fusion.44
  171.1 0.1 fusion.53
  171.2 0.1 fusion.50
  171.3 52.0 %all-gather.4.cloned.1.call-done = f32[16,2,6,8,8,128]{5,4,3,2,1,0:T(8,128)} async-done(((f32[1,2,6,8,8,128]{5,4,3,2,1,0:T(8,128)}), f32[16,2,6,8,8,128]{5,4,3,2,1,0:T(8,128)}) %all-gather.4.cloned.1.call-update) | async-done | bytes 6291472 | tf_op jit(solution)/shard_map/all_gather | solution.py:151
  223.3 9.6 %fusion = f32[1,2,6,8,8,128]{5,0,4,3,2,1:T(1,128)S(1)} fusion(f32[16,2,6,8,8,128]{5,4,3,2,1,0:T(8,128)} %all-gather.4.cloned.1.call-done, s32[]{:T(128)S(6)} %axis_index.15), kind=kOutput, calls=%fused_computation | convolution fusion | flops 18874928 | bytes 6684676 | tf_op jit(solution)/shard_map/dot_general | solution.py:154
  232.9 1.0 subtract_bitcast_fusion
  (88 shorter events, 2.2 us)
Async XLA Ops:
  7.2 31.2 %copy-start.6 = (f32[6]{0:T(128)S(1)}, f32[6]{0:T(128)}, u32[]{:S(2)}) copy-start(f32[6]{0:T(128)} %constant.131.clone) | copy-start | bytes 76
  7.2 30.6 %copy-start = (f32[1,2,6,8,8,128]{5,4,3,2,1,0:T(8,128)S(1)}, f32[1,2,6,8,8,128]{5,4,3,2,1,0:T(8,128)}, u32[]{:S(2)}) copy-start(f32[1,2,6,8,8,128]{5,4,3,2,1,0:T(8,128)} %param.5) | copy-start | bytes 1179652
  7.2 159.7 %all-gather.6.cloned.1.call-start = ((), (), s32[]{:S(2)}) async-start(), calls=%async_computation.2 | async-start | bytes 1622016 | tf_op jit(solution)/shard_map/all_gather | solution.py:143
  8.8 214.5 %all-gather.4.cloned.1.call-start = ((), (), s32[]{:S(2)}) async-start(), calls=%async_computation.1 | async-start | bytes 6684672 | tf_op jit(solution)/shard_map/all_gather | solution.py:151
  10.8 42.1 %collective-permute-start = (f32[1,2,6,8,8,2]{5,4,3,2,1,0:T(8,128)S(1)}, f32[1,2,6,8,8,2]{5,4,3,2,1,0:T(8,128)}, u32[]{:S(2)}, u32[]{:S(2)}) collective-permute-start(f32[1,2,6,8,8,2]{5,4,3,2,1,0:T(8,128)S(1)} %get-tuple-element.69), channel_id=1, source_target_pairs={{0,1},{1,2},{2,3},{3,4},{4,5},{5,6},{6,7},{7,8},{8,9},{9,10},{10,1... | collective-permute-start | bytes 18440 | tf_op jit(solution)/shard_map/ppermute | solution.py:20
  16.4 36.4 %collective-permute-start.1 = (f32[1,2,6,8,8,2]{5,4,3,2,1,0:T(8,128)S(1)}, f32[1,2,6,8,8,2]{5,4,3,2,1,0:T(8,128)}, u32[]{:S(2)}, u32[]{:S(2)}) collective-permute-start(f32[1,2,6,8,8,2]{5,4,3,2,1,0:T(8,128)S(1)} %get-tuple-element.70), channel_id=1, source_target_pairs={{1,0},{2,1},{3,2},{4,3},{5,4},{6,5},{7,6},{8,7},{9,8},{10,9},{11,1... | collective-permute-start | bytes 18440 | tf_op jit(solution)/shard_map/ppermute | solution.py:23
  28.7 11.3 %copy-start.4 = (s32[1,2,1]{1,2,0:T(1,128)S(1)}, s32[1,2,1]{1,2,0:T(1,128)}, u32[]{:S(2)}) copy-start(s32[1,2,1]{1,2,0:T(1,128)} %param.6) | copy-start | bytes 28
  28.7 139.7 %all-to-all-start = ((f32[32,1,6,2,8,128]{5,4,3,2,1,0:T(8,128)}), f32[32,1,6,2,8,128]{5,4,3,2,1,0:T(8,128)S(1)}, u32[]{:S(2)}, u32[]{:S(2)}) async-start(f32[32,1,6,2,8,128]{5,4,3,2,1,0:T(8,128)} %stack.24), calls=%async_computation | async-start | bytes 3145728 | tf_op jit(solution)/shard_map/all_to_all | solution.py:133
  37.8 4.3 %copy-start.5 = (s32[1,2,1]{1,2,0:T(1,128)S(1)}, s32[1,2,1]{1,2,0:T(1,128)}, u32[]{:S(2)}) copy-start(s32[1,2,1]{1,2,0:T(1,128)} %param.7) | copy-start | bytes 28
  168.4 2.5 %copy-start.3 = (f32[6,1,8,128]{3,2,1,0:T(8,128)S(1)}, f32[6,1,8,128]{3,2,1,0:T(8,128)}, u32[]{:S(2)}) copy-start(f32[6,1,8,128]{3,2,1,0:T(8,128)} %slice.761) | copy-start | bytes 73732
  168.4 2.8 %copy-start.1 = (f32[6,8,9,128]{3,2,1,0:T(8,128)S(1)}, f32[6,8,9,128]{3,2,1,0:T(8,128)}, u32[]{:S(2)}) copy-start(f32[6,8,9,128]{3,2,1,0:T(8,128)} %fusion.12) | copy-start | bytes 663556
  169.9 63.1 %copy-start.2 = (f32[2,8,8,128]{3,2,1,0:T(8,128)S(1)}, f32[2,8,8,128]{3,2,1,0:T(8,128)}, u32[]{:S(2)}) copy-start(f32[2,8,8,128]{3,2,1,0:T(8,128)} %fusion.111) | copy-start | bytes 196612
Sparse Core Ops, SparseCore 0:
  11.1 155.7 all-gather.5
  169.0 54.2 all-gather.3
